TPU v7x, 512 devices: a whole 4x4x16 slice. The times are simulated.
512 devices in a mesh: ctx: 64 (over z, y_lo, core), head: 8 (over x, y_hi).
Axes of the slice: x: 4, y: 4 (y_hi: 2, y_lo: 2; y = y_hi * 2 + y_lo), z: 16, core: 2. Of those that a mesh axis runs over, the one named last changes fastest.
Arguments:
- queries_nope: bfloat16 [4096, 8192], P('ctx', 'head'), may hold values from -4 to 4
- queries_rope: bfloat16 [4096, 4096], P('ctx', 'head'), may hold values from -128 to 128
- latents: bfloat16 [4096, 512], P('ctx'), may hold values from -8 to 8
- rope_keys: bfloat16 [4096, 64], P('ctx'), may hold values from -4 to 4
- positions: int32 [4096], P('ctx'), may hold values from 0 to 6143
- key_up: bfloat16 [512, 8192], P(None, 'head'), may hold values from -0.5 to 0.5
- value_up: bfloat16 [512, 8192], P(None, 'head'), may hold values from -0.25 to 0.25
- out_proj: bfloat16 [8192, 3584], P('head', 'ctx'), may hold values from -0.0625 to 0.0625
Outputs:
- attended: bfloat16 [4096, 3584], P('ctx', 'head')
All inputs are finite; a program needn't handle non-finite values.
Results may differ from a plain program's by a relative error of at most 0.014.
The roundings to bfloat16 on the way count: a program that leaves them out, or rounds other values in their place, can miss the bound.
Values may be sent and summed in bfloat16 or wider, within the bound.
No kernel may reach another device: no remote copies, remote signals or barrier semaphores. Data moves between devices by JAX's collectives and lax.ppermute only.
A program may use at most 64 MiB of HBM per device.

v0:
```python
import math
import jax
import jax.numpy as jnp
from jax import lax
from jax.sharding import PartitionSpec as P

LATENT = 512
ROPE = 64
NOPE = 128
VDIM = 128
masked_value = -1e30


def rope_tables(token_pos, width):
    half_width = width // 2
    freqs = jnp.exp(jnp.arange(half_width, dtype=jnp.float32) * (-2.0 * math.log(10000.0) / width))
    angle = token_pos.astype(jnp.float32)[:, None] * freqs[None, :]
    return (jnp.cos(angle), jnp.sin(angle))


def rotate(values, cosine, sine):
    half_width = values.shape[-1] // 2
    first_half = values[..., :half_width]
    second_half = values[..., half_width:]
    cos_part = cosine[:, None, :]
    sin_part = sine[:, None, :]
    return jnp.concatenate(
        [
            first_half * cos_part - second_half * sin_part,
            second_half * cos_part + first_half * sin_part,
        ],
        axis=-1,
    )


def make_update(group, keys, rope_part, key_pos):
    lat_query, rope_query, query_pos = group
    scale = 1.0 / math.sqrt(NOPE + ROPE)

    def update(state):
        peak, totals, summed = state
        scores = jnp.einsum("rl,kl->rk", lat_query, keys, preferred_element_type=jnp.float32)
        scores = scores + jnp.einsum(
            "rl,kl->rk", rope_query, rope_part, preferred_element_type=jnp.float32
        )
        visible = key_pos[None, :] <= query_pos[:, None]
        scores = jnp.where(visible, scores * scale, masked_value)
        new_peak = jnp.maximum(peak, jnp.max(scores, axis=1))
        weights = jnp.where(visible, jnp.exp(scores - new_peak[:, None]), 0.0)
        totals = jnp.sum(weights, axis=1)
        summed = jnp.dot(weights.astype(jnp.bfloat16), keys, preferred_element_type=jnp.float32)
        return (new_peak, totals, summed)

    return update


def unchanged(state):
    return state


def attend(groups, latents, rot_keys, positions):
    initial = tuple(
        (
            (
                jnp.full((group[0].shape[0],), masked_value, jnp.float32),
                jnp.zeros((group[0].shape[0],), jnp.float32),
                jnp.zeros((group[0].shape[0], LATENT), jnp.float32),
            )
            for group in groups
        )
    )
    keys = lax.all_gather(latents, "ctx", axis=0, tiled=True)
    rope_part = lax.all_gather(rot_keys, "ctx", axis=0, tiled=True)
    key_pos = lax.all_gather(positions, "ctx", axis=0, tiled=True)
    earliest = jnp.min(key_pos)
    results = []
    for group, fold_state in zip(groups, initial):
        needed = earliest <= jnp.max(group[2])
        results.append(
            lax.cond(needed, make_update(group, keys, rope_part, key_pos), unchanged, fold_state)
        )
    states = tuple(results)
    return [(state[2] / state[1][:, None]).astype(jnp.bfloat16) for state in states]


def upward(latent_out, value_up, token_count, head_count):
    head_out = jnp.einsum(
        "thl,lhd->thd",
        latent_out.reshape(token_count, head_count, LATENT),
        value_up.reshape(LATENT, head_count, VDIM),
        preferred_element_type=jnp.float32,
    )
    return head_out.astype(jnp.bfloat16).reshape(token_count, head_count * VDIM)


def body(queries_nope, queries_rope, latents, rope_keys, positions, key_up, value_up, out_proj):
    token_count = latents.shape[0]
    head_count = key_up.shape[1] // NOPE
    cosine, sine = rope_tables(positions, ROPE)
    rot_queries = rotate(
        queries_rope.astype(jnp.float32).reshape(token_count, head_count, ROPE), cosine, sine
    ).astype(jnp.bfloat16)
    rot_keys = rotate(rope_keys.astype(jnp.float32)[:, None, :], cosine, sine)[:, 0, :].astype(
        jnp.bfloat16
    )
    lat_queries = jnp.einsum(
        "thn,lhn->thl",
        queries_nope.reshape(token_count, head_count, NOPE),
        key_up.reshape(LATENT, head_count, NOPE),
        preferred_element_type=jnp.float32,
    ).astype(jnp.bfloat16)
    lat_rows = lat_queries.reshape(token_count * head_count, LATENT)
    rope_rows = rot_queries.reshape(token_count * head_count, ROPE)
    groups = [(lat_rows, rope_rows, jnp.repeat(positions, head_count))]
    outcome = attend(groups, latents, rot_keys, positions)
    head_out = upward(outcome[0], value_up, token_count, head_count)
    partial_sums = jnp.dot(
        head_out,
        lax.all_gather(out_proj, "ctx", axis=1, tiled=True),
        preferred_element_type=jnp.float32,
    )
    return lax.psum_scatter(
        partial_sums.astype(jnp.bfloat16), "head", scatter_dimension=1, tiled=True
    )


def solution(mesh):
    in_specs = (
        P("ctx", "head"),
        P("ctx", "head"),
        P("ctx", None),
        P("ctx", None),
        P("ctx"),
        P(None, "head"),
        P(None, "head"),
        P("head", "ctx"),
    )
    out_specs = P("ctx", "head")
    return jax.shard_map(body, mesh=mesh, in_specs=in_specs, out_specs=out_specs, check_vma=False)
```

profile of v0, /device:TPU:2, one launch (start us, length us, event | category | flops | bytes accessed | tf_op | source)
XLA Modules:
  0.0 420.3 jit_solution(58696167406577907)
XLA Ops:
  6.5 0.7 all-gather.4.cloned.1.call-update
  7.3 0.7 all-gather.6.cloned.1.call-update
  8.0 0.0 reduce-scatter.4.cloned.1.call-start
  8.1 0.7 convert_element_type.38
  8.7 1.0 reshape.142
  9.7 0.8 copy.44
  10.5 0.1 fusion.31
  10.7 0.1 copy.45
  10.8 75.8 %all-gather = bf16[4096,1,64]{2,1,0:T(2,128)(2,1)S(1)} all-gather(bf16[64,1,64]{2,1,0:T(2,128)(2,1)S(1)} %copy.45), channel_id=2, replica_groups=mesh['ctx'=64,'head'=8] {'ctx'}, dimensions={0}, use_global_device_ids=true | all-gather | bytes 532480 | tf_op jit(solution)/shard_map/all_gather | solution.py:73
  86.6 3.6 copy.46
  90.2 1.3 dynamic-slice
  92.1 0.9 dynamic-update-slice
  93.0 208.6 %all-reduce = s32[4096]{0:T(1024)S(1)} all-reduce(s32[4096]{0:T(1024)S(1)} %dynamic-update-slice), channel_id=1, replica_groups=mesh['ctx'=64,'head'=8] {'ctx'}, use_global_device_ids=true, to_apply=%add | all-reduce | flops 4096 | bytes 32768
  301.6 0.6 reduce_min.9
  302.2 1.4 broadcast_reduce_fusion
  305.0 0.2 multiply_cosine_fusion
  305.2 0.2 fusion.20
  305.4 0.1 pad_maximum_fusion
  305.5 1.4 fusion.12
  306.9 0.1 broadcast_in_dim.34
  307.0 11.8 %conditional.1 = (f32[512]{0:T(512)S(1)}, f32[512,512]{1,0:T(8,128)S(1)}) conditional(s32[]{:T(128)} %convert_element_type.35, () %tuple.13, (s32[4096]{0:T(1024)S(1)}, s32[64,8]{1,0:T(8,128)S(1)}, bf16[64,8,512]{2,0,1:T(8,128)(2,1)S(1)}, bf16[4096,512]{1,0:T(8,128)(2,1)}, bf16[512,64]{1,0:T(8,128)(2,1)S(1)}, ...), branch_computations={%region_2.0_spmd, %region_3.6_spmd} | conditional | flops 4590665216 | bytes 71440456 | solution.py:80
  307.0 0.1 le.3
  307.1 4.7 %fusion.8 = f32[512,4096]{1,0:T(8,128)S(1)} fusion(bf16[4096,512]{1,0:T(8,128)(2,1)} %get-tuple-element.21, bf16[64,8,512]{2,0,1:T(8,128)(2,1)S(1)} %get-tuple-element.60), kind=kOutput, calls=%fused_computation.9 | convolution fusion | flops 2147483648 | bytes 13107200 | tf_op jit(solution)/shard_map/cond/branch_1_fun/rl,kl->rk/dot_general | solution.py:42
  311.8 2.2 fusion.34
  314.0 2.4 fusion.2
  316.4 2.2 fusion.1
  318.8 0.1 fusion.19
  318.9 1.7 fusion.13
  320.7 5.4 %convolution_convert_fusion = bf16[64,3584]{1,0:T(8,128)(2,1)S(1)} fusion(bf16[1024,3584]{0,1:T(8,128)(2,1)} %all-gather.6.cloned.1.call-done, bf16[8,8,8,128]{3,2,1,0:T(8,128)(2,1)S(1)} %fusion.13), kind=kOutput, calls=%fused_computation.14 | convolution fusion | flops 469991424 | bytes 7929856 | tf_op jit(solution)/shard_map/dot_general | solution.py:117
  326.1 1.2 copy.53
  327.4 84.8 %reduce-scatter.4.cloned.1.call-done = bf16[448,64]{1,0:T(8,128)(2,1)} async-done(((bf16[3584,64]{1,0:T(8,128)(2,1)}), bf16[448,64]{1,0:T(8,128)(2,1)}) %reduce-scatter.4.cloned.1.call-update) | async-done | bytes 57360
  412.2 1.6 copy.54
  (18 shorter events, 0.1 us)
Async XLA Ops:
  6.5 298.9 %copy-start = (bf16[512,1024]{1,0:T(8,128)(2,1)S(1)}, bf16[512,1024]{1,0:T(8,128)(2,1)}, u32[]{:S(2)}) copy-start(bf16[512,1024]{1,0:T(8,128)(2,1)} %param.15) | copy-start | bytes 3145732
  6.5 300.4 %copy-start.3 = (s32[64]{0:T(128)S(1)}, s32[64]{0:T(128)}, u32[]{:S(2)}) copy-start(s32[64]{0:T(128)} %param.14) | copy-start | bytes 772
  6.5 300.4 %all-gather.4.cloned.1.call-start = ((), (), s32[]{:S(2)}) async-start(), calls=%async_computation.1 | async-start | bytes 4259840 | tf_op jit(solution)/shard_map/all_gather | solution.py:72
  7.3 313.4 %all-gather.6.cloned.1.call-start = ((), (), s32[]{:S(2)}) async-start(), calls=%async_computation.2 | async-start | bytes 7454720 | tf_op jit(solution)/shard_map/all_gather | solution.py:119
  8.0 404.2 %reduce-scatter.4.cloned.1.call-start = ((), (), s32[]{:S(2)}) async-start(), calls=%async_computation.3 | async-start | bytes 1032192
  307.0 4.8 %copy-start.2 = (bf16[4096,64]{0,1:T(8,128)(2,1)S(1)}, bf16[4096,64]{0,1:T(8,128)(2,1)}, u32[]{:S(2)}) copy-start(bf16[4096,64]{0,1:T(8,128)(2,1)} %get-tuple-element.63) | copy-start | bytes 1572868 | tf_op jit(solution)/shard_map/cond
  311.8 2.2 copy-start.1
Sparse Core Ops, SparseCore 0:
  9.5 128.9 all-gather.3
  140.7 124.4 all-gather.5
  327.5 84.6 reduce-scatter.3
where the time goes:
time: 421 us; the launch traced here: 420 us
  blocking collectives  284 us (67%)
  waiting for transfers between devices  86.3 us (20%)
  matrix products  17.8 us (4%)
  between operations  15.2 us (4%)
  local copies, waits for them, and re-layouts  10.6 us (3%)
  other arithmetic  5.75 us (1%)
    unnamed x1, blocking collectives  209 us
    unnamed x4, waiting for transfers between devices  86.2 us
    all_gather x1, blocking collectives, attend(): rope_part = lax.all_gather(rot_keys, 'ctx', axis=0, tiled=True)  75.8 us
  transfers between devices with their start and end apart: 3, of which 1 were waited for; matrix products, arithmetic and copies ran while one was open for 6% of the time, Pallas kernels for 0%

commit v1 on v0

--- a/solution.py
+++ b/solution.py
@@ -70,7 +70,10 @@
         )
     )
     keys = lax.all_gather(latents, "ctx", axis=0, tiled=True)
-    rope_part = lax.all_gather(rot_keys, "ctx", axis=0, tiled=True)
+    size = lax.axis_size("ctx")
+    blocks = jnp.stack([rot_keys for _ in range(size)])
+    blocks = lax.all_to_all(blocks, "ctx", split_axis=0, concat_axis=0)
+    rope_part = jnp.concatenate(blocks, axis=0)
     key_pos = lax.all_gather(positions, "ctx", axis=0, tiled=True)
     earliest = jnp.min(key_pos)
     results = []

time: 421 us -> 384 us (0.912)
  blocking collectives: 284 us -> 223 us
  starting transfers between devices: 0.08 us -> 17.2 us
  waiting for transfers between devices: 86.3 us -> 95.2 us
    all_gather x1 -> x0, blocking collectives: 75.8 us -> none  [attend(): rope_part = lax.all_gather(rot_keys, 'ctx', axis=0, tiled=True)]
    all_to_all x0 -> x1, starting transfers between devices: none -> 17.1 us  [attend(): blocks = lax.all_to_all(blocks, 'ctx', split_axis=0, concat_axis=0)]
    unnamed x1, blocking collectives: 209 us -> 223 us
    unnamed x4, waiting for transfers between devices: 86.2 us -> 95.2 us
  transfers between devices with their start and end apart: 3 -> 4, of which waited for: 1 -> 1; matrix products, arithmetic and copies ran while one was open for 6% -> 6% of each run, Pallas kernels for 0% -> 0%
where the time goes in v1:
time: 384 us
  blocking collectives  223 us (58%)
  waiting for transfers between devices  95.2 us (25%)
  matrix products  17.7 us (5%)
  starting transfers between devices  17.2 us (4%)
  between operations  15.2 us (4%)
  local copies, waits for them, and re-layouts  9.57 us (2%)
  other arithmetic  5.69 us (1%)
    unnamed x1, blocking collectives  223 us
    unnamed x4, waiting for transfers between devices  95.2 us
    all_to_all x1, starting transfers between devices, attend(): blocks = lax.all_to_all(blocks, 'ctx', split_axis=0, concat_axis=0)  17.1 us
    unnamed x12, local copies, waits for them, and re-layouts  8.02 us
  transfers between devices with their start and end apart: 4, of which 1 were waited for; matrix products, arithmetic and copies ran while one was open for 6% of the time, Pallas kernels for 0%

profile of v1, /device:TPU:2, one launch (start us, length us, event | category | flops | bytes accessed | tf_op | source)
XLA Modules:
  0.0 383.6 jit_solution(9646696965460987193)
XLA Ops:
  6.5 0.7 all-gather.3.cloned.1.call-update
  7.3 0.7 all-gather.5.cloned.1.call-update
  8.0 0.7 convert_element_type.40
  8.7 0.8 copy.28
  9.5 0.1 fusion.31
  9.7 0.1 copy.29
  9.8 0.3 stack.2
  10.0 1.5 reshape.158
  11.6 17.1 %all-to-all-start = ((bf16[64,2,2048]{2,1,0:T(2,128)(2,1)}), bf16[64,2,2048]{2,1,0:T(2,128)(2,1)S(1)}, u32[]{:S(2)}, u32[]{:S(2)}) async-start(bf16[64,2,2048]{2,1,0:T(2,128)(2,1)} %reshape.158), calls=%async_computation | async-start | bytes 1048576 | tf_op jit(solution)/shard_map/all_to_all | solution.py:75
  28.7 1.0 reshape.150
  29.7 1.3 dynamic-slice
  31.7 0.9 dynamic-update-slice
  32.5 222.9 %all-reduce = s32[4096]{0:T(1024)S(1)} all-reduce(s32[4096]{0:T(1024)S(1)} %dynamic-update-slice), channel_id=1, replica_groups=mesh['ctx'=64,'head'=8] {'ctx'}, use_global_device_ids=true, to_apply=%add | all-reduce | flops 4096 | bytes 32768
  255.4 0.6 reduce_min.9
  256.0 1.4 broadcast_reduce_fusion
  258.7 0.2 multiply_cosine_fusion
  258.9 0.2 fusion.20
  259.1 0.1 pad_maximum_fusion
  259.2 1.4 fusion.12
  260.6 0.7 reshape.159
  261.4 11.7 %conditional.1 = (f32[512]{0:T(512)S(1)}, f32[512,512]{1,0:T(8,128)S(1)}) conditional(s32[]{:T(128)} %convert_element_type.37, () %tuple.13, (s32[4096]{0:T(1024)S(1)}, s32[64,8]{1,0:T(8,128)S(1)}, bf16[64,8,512]{2,0,1:T(8,128)(2,1)S(1)}, bf16[4096,512]{1,0:T(8,128)(2,1)}, bf16[64,64,64]{2,1,0:T(8,128)(2,1)S(1)}, ...), branch_computations={%region_2.0_spmd, %region_3.6_spmd} | conditional | flops 4590665216 | bytes 69343280 | solution.py:83
  261.4 0.1 le.3
  261.5 4.6 %fusion.8 = f32[512,4096]{1,0:T(8,128)S(1)} fusion(bf16[4096,512]{1,0:T(8,128)(2,1)} %get-tuple-element.22, bf16[64,8,512]{2,0,1:T(8,128)(2,1)S(1)} %get-tuple-element.49), kind=kOutput, calls=%fused_computation.9 | convolution fusion | flops 2147483648 | bytes 13107200 | tf_op jit(solution)/shard_map/cond/branch_1_fun/rl,kl->rk/dot_general | solution.py:42
  266.1 2.1 fusion.34
  268.3 2.4 fusion.2
  270.7 2.2 fusion.1
  273.1 0.1 fusion.19
  273.3 1.7 fusion.13
  275.0 5.4 %convolution_convert_fusion = bf16[64,3584]{1,0:T(8,128)(2,1)S(1)} fusion(bf16[1024,3584]{0,1:T(8,128)(2,1)} %all-gather.5.cloned.1.call-done, bf16[8,8,8,128]{3,2,1,0:T(8,128)(2,1)S(1)} %fusion.13), kind=kOutput, calls=%fused_computation.14 | convolution fusion | flops 469991424 | bytes 7929856 | tf_op jit(solution)/shard_map/dot_general | solution.py:120
  280.4 1.2 copy.34
  281.7 93.8 %reduce-scatter.4.cloned.1.call-done = bf16[448,64]{1,0:T(8,128)(2,1)} async-done(((bf16[3584,64]{1,0:T(8,128)(2,1)}), bf16[448,64]{1,0:T(8,128)(2,1)}) %reduce-scatter.4.cloned.1.call-update) | async-done | bytes 57360
  375.5 1.6 copy.35
  (19 shorter events, 0.3 us)
Async XLA Ops:
  6.5 252.6 %copy-start = (bf16[512,1024]{1,0:T(8,128)(2,1)S(1)}, bf16[512,1024]{1,0:T(8,128)(2,1)}, u32[]{:S(2)}) copy-start(bf16[512,1024]{1,0:T(8,128)(2,1)} %param.15) | copy-start | bytes 3145732
  6.5 254.8 %copy-start.2 = (s32[64]{0:T(128)S(1)}, s32[64]{0:T(128)}, u32[]{:S(2)}) copy-start(s32[64]{0:T(128)} %param.14) | copy-start | bytes 772
  6.5 254.7 %all-gather.3.cloned.1.call-start = ((), (), s32[]{:S(2)}) async-start(), calls=%async_computation.2 | async-start | bytes 4259840 | tf_op jit(solution)/shard_map/all_gather | solution.py:72
  7.3 267.7 %all-gather.5.cloned.1.call-start = ((), (), s32[]{:S(2)}) async-start(), calls=%async_computation.3 | async-start | bytes 7454720 | tf_op jit(solution)/shard_map/all_gather | solution.py:122
  11.6 249.0 %all-to-all-start = ((bf16[64,2,2048]{2,1,0:T(2,128)(2,1)}), bf16[64,2,2048]{2,1,0:T(2,128)(2,1)S(1)}, u32[]{:S(2)}, u32[]{:S(2)}) async-start(bf16[64,2,2048]{2,1,0:T(2,128)(2,1)} %reshape.158), calls=%async_computation | async-start | bytes 1048576 | tf_op jit(solution)/shard_map/all_to_all | solution.py:75
  28.7 346.8 %reduce-scatter.4.cloned.1.call-start = ((), (), s32[]{:S(2)}) async-start(), calls=%async_computation.4 | async-start | bytes 1032192
  266.1 2.2 copy-start.1
Sparse Core Ops, SparseCore 0:
  9.5 136.9 all-gather.2
  148.6 124.4 all-gather.4
  281.8 93.5 reduce-scatter.3
